TPU v7x, 32 devices: a whole 2x2x4 slice. The times are simulated.
32 devices in a mesh: src: 8 (over z, y), vox: 4 (over x, core).
Axes of the slice: x: 2, y: 2, z: 4, core: 2. Of those that a mesh axis runs over, the one named last changes fastest.
Arguments:
- forward_voxel_field: bfloat16 [4096, 4096], P('src', 'vox'), may hold values from -0.09375 to 0.09375
- adjoint_voxel_field: bfloat16 [4096, 4096], P('src', 'vox'), may hold values from -6 to 6
- voxel_input_vector: float32 [4096], P('vox'), may hold values from -6 to 6
- measurement_weight: float32 [4096, 4096], P('src', 'vox'), may hold values from 0.00390625 to 0.0390625
Outputs:
- hess_vector: float32 [4096], P('vox')
All inputs are finite; a program needn't handle non-finite values.
Results may differ from a plain program's by a relative error of at most 0.00056.
Values may be sent and summed in bfloat16 or wider, within the bound.
No kernel may reach another device: no remote copies, remote signals or barrier semaphores. Data moves between devices by JAX's collectives and lax.ppermute only.
A program may use at most 64 MiB of HBM per device.

v0:
```python
import jax
import jax.numpy as jnp
from jax import lax
from jax.sharding import PartitionSpec as P


def per_device(forward_voxel_field, adjoint_voxel_field, voxel_input_vector, measurement_weight):
    scaled = (forward_voxel_field.astype(jnp.float32) * voxel_input_vector[None, :]).astype(
        jnp.bfloat16
    )
    adjoint_all = lax.all_gather(adjoint_voxel_field, "src", axis=0, tiled=True)
    predicted_part = lax.dot_general(
        scaled, adjoint_all, (((1,), (1,)), ((), ())), preferred_element_type=jnp.float32
    )
    pred_share = lax.psum_scatter(predicted_part, "vox", scatter_dimension=1, tiled=True)
    weighted_share = (measurement_weight * pred_share).astype(jnp.bfloat16)
    weighted_signal = lax.all_gather(weighted_share, "vox", axis=1, tiled=True)
    back = jnp.dot(weighted_signal, adjoint_all, preferred_element_type=jnp.float32)
    local_sum = jnp.sum(forward_voxel_field.astype(jnp.float32) * back, axis=0)
    return lax.psum(local_sum, "src")


def solution(mesh):
    placed = (P("src", "vox"), P("src", "vox"), P("vox"), P("src", "vox"))
    return jax.shard_map(
        per_device, mesh=mesh, in_specs=placed, out_specs=P("vox"), check_vma=False
    )
```

profile of v0, /device:TPU:0, one launch (start us, length us, event | category | flops | bytes accessed | tf_op | source)
XLA Modules:
  0.0 294.0 jit_solution(4092530594951713219)
XLA Ops:
  6.5 0.0 all-gather.3.cloned.1.call-start
  6.5 0.7 all-gather.3.cloned.1.call-update
  7.3 0.0 reduce-scatter.2.cloned.1.call-start
  7.3 129.8 %all-gather.3.cloned.1.call-done = bf16[4096,1024]{1,0:T(8,128)(2,1)} async-done(((bf16[512,1024]{1,0:T(8,128)(2,1)}), bf16[4096,1024]{1,0:T(8,128)(2,1)}) %all-gather.3.cloned.1.call-update) | async-done | bytes 8388624 | tf_op jit(solution)/shard_map/all_gather | solution.py:11
  137.2 11.5 %fusion.2 = f32[512,4096]{1,0:T(8,128)} fusion(bf16[4096,1024]{1,0:T(8,128)(2,1)} %all-gather.3.cloned.1.call-done, bf16[512,1024]{1,0:T(8,128)(2,1)} %param.4, f32[1024]{0:T(1024)} %param.6), kind=kOutput, calls=%fused_computation.5 | convolution fusion | flops 4296540160 | bytes 17829888 | tf_op jit(solution)/shard_map/dot_general | solution.py:12
  148.7 0.0 copy-start
  148.7 0.0 reduce-scatter.2.cloned.1.call-update
  148.7 0.0 copy-start.1
  148.7 0.0 all-gather.5.cloned.1.call-start
  148.7 70.0 %reduce-scatter.2.cloned.1.call-done = f32[512,1024]{1,0:T(8,128)} async-done(((f32[512,4096]{1,0:T(8,128)}), f32[512,1024]{1,0:T(8,128)}) %reduce-scatter.2.cloned.1.call-update) | async-done | bytes 2097168 | tf_op jit(solution)/shard_map/reduce_scatter | solution.py:15
  218.7 0.0 copy-done
  218.7 2.9 multiply_convert_fusion
  221.7 0.0 all-gather.5.cloned.1.call-update
  221.7 34.6 %all-gather.5.cloned.1.call-done = bf16[512,4096]{1,0:T(8,128)(2,1)} async-done(((bf16[512,1024]{1,0:T(8,128)(2,1)}), bf16[512,4096]{1,0:T(8,128)(2,1)}) %all-gather.5.cloned.1.call-update) | async-done | bytes 4194320 | tf_op jit(solution)/shard_map/all_gather | solution.py:17
  256.3 0.0 copy-done.1
  256.3 9.2 %fusion.1 = f32[1024]{0:T(1024)S(1)} fusion(bf16[512,1024]{1,0:T(8,128)(2,1)S(1)} %copy-done.1, bf16[512,4096]{1,0:T(8,128)(2,1)} %all-gather.5.cloned.1.call-done, bf16[4096,1024]{1,0:T(8,128)(2,1)} %all-gather.3.cloned.1.call-done), kind=kOutput, calls=%fused_computation.3 | convolution fusion | flops 4296539136 | bytes 13635584 | tf_op jit(solution)/shard_map/dot_general | solution.py:18
  265.5 22.0 %psum.7 = f32[1024]{0:T(1024)} all-reduce(f32[1024]{0:T(1024)S(1)} %fusion.1), channel_id=1, replica_groups=mesh['src'=8,'vox'=4] {'src'}, use_global_device_ids=true, to_apply=%region_2.0 | all-reduce | flops 1024 | bytes 8192 | tf_op jit(solution)/shard_map/psum | solution.py:20
Async XLA Ops:
  6.5 130.6 %all-gather.3.cloned.1.call-start = ((), (), s32[]{:S(2)}) async-start(), calls=%async_computation.1 | async-start | bytes 9437184 | tf_op jit(solution)/shard_map/all_gather | solution.py:11
  7.3 211.5 %reduce-scatter.2.cloned.1.call-start = ((), (), s32[]{:S(2)}) async-start(), calls=%async_computation.2 | async-start | bytes 10485760 | tf_op jit(solution)/shard_map/reduce_scatter | solution.py:15
  148.7 70.1 %copy-start = (f32[512,1024]{1,0:T(8,128)S(1)}, f32[512,1024]{1,0:T(8,128)}, u32[]{:S(2)}) copy-start(f32[512,1024]{1,0:T(8,128)} %param.7) | copy-start | bytes 6291460
  148.7 107.7 %copy-start.1 = (bf16[512,1024]{1,0:T(8,128)(2,1)S(1)}, bf16[512,1024]{1,0:T(8,128)(2,1)}, u32[]{:S(2)}) copy-start(bf16[512,1024]{1,0:T(8,128)(2,1)} %param.4) | copy-start | bytes 3145732
  148.7 107.6 %all-gather.5.cloned.1.call-start = ((), (), s32[]{:S(2)}) async-start(), calls=%async_computation.3 | async-start | bytes 5242880 | tf_op jit(solution)/shard_map/all_gather | solution.py:17
Sparse Core Ops, SparseCore 0:
  9.5 127.6 all-gather.2
  148.8 69.8 reduce-scatter.1
  221.8 34.4 all-gather.4
where the time goes:
time: 294 us
  waiting for transfers between devices  235 us (80%)
  blocking collectives  22 us (7%)
  matrix products  20.7 us (7%)
  between operations  13.1 us (4%)
    all_gather x1, waiting for transfers between devices, per_device(): adjoint_all = lax.all_gather(adjoint_voxel_field, 'src', axis=0, tiled=True)  130 us
    reduce_scatter x1, waiting for transfers between devices, per_device(): lax.psum_scatter(predicted_part, 'vox', scatter_dimension=1, tiled=True)  70 us
    all_gather x1, waiting for transfers between devices, per_device(): weighted_signal = lax.all_gather(weighted_share, 'vox', axis=1, tiled=True)  34.6 us
    psum x1, blocking collectives, per_device(): return lax.psum(local_sum, 'src')  22 us
    dot_general x1, matrix products, per_device(): lax.dot_general(scaled, adjoint_all, (((1,), (1,)), ((), ())), preferred_...  11.5 us
    dot_general x1, matrix products, per_device(): jnp.dot(weighted_signal, adjoint_all, preferred_element_type=jnp.float32)  9.15 us
  transfers between devices with their start and end apart: 3, of which 3 were waited for; matrix products, arithmetic and copies ran while one was open for 0% of the time, Pallas kernels for 0%

commit v1 on v0

--- a/solution.py
+++ b/solution.py
@@ -17,7 +17,7 @@
     weighted_signal = lax.all_gather(weighted_share, "vox", axis=1, tiled=True)
     back = jnp.dot(weighted_signal, adjoint_all, preferred_element_type=jnp.float32)
     local_sum = jnp.sum(forward_voxel_field.astype(jnp.float32) * back, axis=0)
-    return lax.psum(local_sum, "src")
+    return jnp.sum(lax.all_gather(local_sum, "src"), axis=0)
 
 
 def solution(mesh):

time: 294 us -> 303 us (1.031)
  blocking collectives: 22 us -> 30.5 us
    all_gather x0 -> x1, blocking collectives: none -> 30.5 us  [per_device(): return jnp.sum(lax.all_gather(local_sum, 'src'), axis=0)]
    psum x1 -> x0, blocking collectives: 22 us -> none  [per_device(): return lax.psum(local_sum, 'src')]
where the time goes in v1:
time: 303 us
  waiting for transfers between devices  235 us (78%)
  blocking collectives  30.5 us (10%)
  matrix products  20.7 us (7%)
  between operations  13.1 us (4%)
  other arithmetic  3.53 us (1%)
    all_gather x1, waiting for transfers between devices, per_device(): adjoint_all = lax.all_gather(adjoint_voxel_field, 'src', axis=0, tiled=True)  130 us
    reduce_scatter x1, waiting for transfers between devices, per_device(): lax.psum_scatter(predicted_part, 'vox', scatter_dimension=1, tiled=True)  70 us
    all_gather x1, waiting for transfers between devices, per_device(): weighted_signal = lax.all_gather(weighted_share, 'vox', axis=1, tiled=True)  34.6 us
    all_gather x1, blocking collectives, per_device(): return jnp.sum(lax.all_gather(local_sum, 'src'), axis=0)  30.5 us
    dot_general x1, matrix products, per_device(): lax.dot_general(scaled, adjoint_all, (((1,), (1,)), ((), ())), preferred_...  11.5 us
    dot_general x1, matrix products, per_device(): jnp.dot(weighted_signal, adjoint_all, preferred_element_type=jnp.float32)  9.15 us
  transfers between devices with their start and end apart: 3, of which 3 were waited for; matrix products, arithmetic and copies ran while one was open for 0% of the time, Pallas kernels for 0%

profile of v1, /device:TPU:0, one launch (start us, length us, event | category | flops | bytes accessed | tf_op | source)
XLA Modules:
  0.0 303.1 jit_solution(7315946149161899780)
XLA Ops:
  6.5 0.0 all-gather.4.cloned.1.call-start
  6.5 0.7 all-gather.4.cloned.1.call-update
  7.3 0.0 reduce-scatter.2.cloned.1.call-start
  7.3 129.8 %all-gather.4.cloned.1.call-done = bf16[4096,1024]{1,0:T(8,128)(2,1)} async-done(((bf16[512,1024]{1,0:T(8,128)(2,1)}), bf16[4096,1024]{1,0:T(8,128)(2,1)}) %all-gather.4.cloned.1.call-update) | async-done | bytes 8388624 | tf_op jit(solution)/shard_map/all_gather | solution.py:11
  137.2 11.5 %fusion.2 = f32[512,4096]{1,0:T(8,128)} fusion(bf16[4096,1024]{1,0:T(8,128)(2,1)} %all-gather.4.cloned.1.call-done, bf16[512,1024]{1,0:T(8,128)(2,1)} %param.4, f32[1024]{0:T(1024)} %param.6), kind=kOutput, calls=%fused_computation.5 | convolution fusion | flops 4296540160 | bytes 17829888 | tf_op jit(solution)/shard_map/dot_general | solution.py:12
  148.7 0.0 copy-start
  148.7 0.0 reduce-scatter.2.cloned.1.call-update
  148.7 0.0 copy-start.1
  148.7 0.0 all-gather.6.cloned.1.call-start
  148.7 70.0 %reduce-scatter.2.cloned.1.call-done = f32[512,1024]{1,0:T(8,128)} async-done(((f32[512,4096]{1,0:T(8,128)}), f32[512,1024]{1,0:T(8,128)}) %reduce-scatter.2.cloned.1.call-update) | async-done | bytes 2097168 | tf_op jit(solution)/shard_map/reduce_scatter | solution.py:15
  218.7 0.0 copy-done
  218.7 2.9 multiply_convert_fusion
  221.7 0.0 all-gather.6.cloned.1.call-update
  221.7 34.6 %all-gather.6.cloned.1.call-done = bf16[512,4096]{1,0:T(8,128)(2,1)} async-done(((bf16[512,1024]{1,0:T(8,128)(2,1)}), bf16[512,4096]{1,0:T(8,128)(2,1)}) %all-gather.6.cloned.1.call-update) | async-done | bytes 4194320 | tf_op jit(solution)/shard_map/all_gather | solution.py:17
  256.3 0.0 copy-done.1
  256.3 9.2 %fusion.1 = f32[1024]{0:T(1024)S(1)} fusion(bf16[512,1024]{1,0:T(8,128)(2,1)S(1)} %copy-done.1, bf16[512,4096]{1,0:T(8,128)(2,1)} %all-gather.6.cloned.1.call-done, bf16[4096,1024]{1,0:T(8,128)(2,1)} %all-gather.4.cloned.1.call-done), kind=kOutput, calls=%fused_computation.3 | convolution fusion | flops 4296539136 | bytes 13635584 | tf_op jit(solution)/shard_map/dot_general | solution.py:18
  265.5 30.5 %all-gather = f32[8192]{0:T(1024)S(1)} all-gather(f32[1024]{0:T(1024)S(1)} %fusion.1), channel_id=2, replica_groups=mesh['src'=8,'vox'=4] {'src'}, dimensions={0}, use_global_device_ids=true | all-gather | bytes 36864 | tf_op jit(solution)/shard_map/all_gather | solution.py:20
  296.0 0.6 reduce_sum.19
  (1 shorter events, 0.0 us)
Async XLA Ops:
  6.5 130.6 %all-gather.4.cloned.1.call-start = ((), (), s32[]{:S(2)}) async-start(), calls=%async_computation.1 | async-start | bytes 9437184 | tf_op jit(solution)/shard_map/all_gather | solution.py:11
  7.3 211.5 %reduce-scatter.2.cloned.1.call-start = ((), (), s32[]{:S(2)}) async-start(), calls=%async_computation.2 | async-start | bytes 10485760 | tf_op jit(solution)/shard_map/reduce_scatter | solution.py:15
  148.7 70.1 %copy-start = (f32[512,1024]{1,0:T(8,128)S(1)}, f32[512,1024]{1,0:T(8,128)}, u32[]{:S(2)}) copy-start(f32[512,1024]{1,0:T(8,128)} %param.7) | copy-start | bytes 6291460
  148.7 107.7 %copy-start.1 = (bf16[512,1024]{1,0:T(8,128)(2,1)S(1)}, bf16[512,1024]{1,0:T(8,128)(2,1)}, u32[]{:S(2)}) copy-start(bf16[512,1024]{1,0:T(8,128)(2,1)} %param.4) | copy-start | bytes 3145732
  148.7 107.6 %all-gather.6.cloned.1.call-start = ((), (), s32[]{:S(2)}) async-start(), calls=%async_computation.3 | async-start | bytes 5242880 | tf_op jit(solution)/shard_map/all_gather | solution.py:17
Sparse Core Ops, SparseCore 0:
  9.5 127.6 all-gather.3
  148.8 69.8 reduce-scatter.1
  221.8 34.4 all-gather.5
